TPU v7x, 512 devices: a whole 4x8x8 slice. The times are simulated.
512 devices in a mesh: src: 32 (over y, x_lo, core), rcv: 8 (over z), int: 2 (over x_hi).
Axes of the slice: x: 4 (x_hi: 2, x_lo: 2; x = x_hi * 2 + x_lo), y: 8, z: 8, core: 2. Of those that a mesh axis runs over, the one named last changes fastest.
Arguments:
- traces: float32 [2, 1, 4096, 4096], P(None, None, 'src', 'rcv'), may hold values from -6 to 6
- missing: int32 [32, 32], P('src', 'rcv'), may hold values from 0 to 1, as said below
- aperture: int32 [32, 24], P('src'), may hold values from 0 to 32, as said below
- wavelet: float32 [2, 1], replicated, may hold values from -0.06 to 0.06
Outputs:
- primaries: float32 [2, 1, 4096, 4096], P(None, None, 'src', ('rcv', 'int'))
Inputs may be any that keep to these rules, and one draw needn't show every extreme that they name: `missing`: A tile is marked only where its receiver block lies above its source block, so the mirrored tile is always recorded; some tile is marked. `aperture`: in each row the listed blocks come first and are distinct; the remaining entries are the padding value 32. Each row lists 24 // 2 to 24 blocks; some row lists exactly 24 and some row exactly 12.
All inputs are finite; a program needn't handle non-finite values.
Results may differ from a plain program's by a relative error of at most 0.00005.
Values sent between devices are 32-bit elements; how exact they have to be, the bound alone decides.
No kernel may reach another device: no remote copies, remote signals or barrier semaphores. Data moves between devices by JAX's collectives and lax.ppermute only.
A program may use at most 64 MiB of HBM per device.

v0:
```python
import jax
import jax.numpy as jnp
from jax import lax
from jax.sharding import PartitionSpec as P

TILE = 128


def from_everyone(x, axis):
    copies = jnp.broadcast_to(x, (lax.axis_size(axis), *x.shape))
    return lax.all_to_all(copies, axis, split_axis=0, concat_axis=0, tiled=True)


def joined_along(pieces, dim):
    pieces = jnp.moveaxis(pieces, 0, dim)
    lengths = pieces.shape
    return pieces.reshape(*lengths[:dim], lengths[dim] * lengths[dim + 1], *lengths[dim + 2 :])


def collect(x, axis, dim):
    pieces = from_everyone(x, axis)
    return joined_along(pieces, dim)


def in_blocks(x, dim, count):
    before, after = (x.shape[:dim], x.shape[dim + 1 :])
    return jnp.moveaxis(x.reshape(*before, count, -1, *after), dim, 0)


def sent_and_summed(x, axis, dim):
    pieces = in_blocks(x, dim, lax.axis_size(axis))
    arrived = lax.all_to_all(pieces, axis, split_axis=0, concat_axis=0, tiled=True)
    return arrived.sum(axis=0)


def complex_prod(left_side, right_side):
    return jnp.einsum("fik,fkj->fij", left_side, right_side, precision=lax.Precision.HIGHEST)


def per_device(traces, missing, aperture, wavelet):
    half_count = lax.axis_size("int")
    my_half = lax.axis_index("int")
    rcv_count = lax.axis_size("rcv")
    comp_count, freq_count, local_rows, local_cols = traces.shape
    regrouped = lax.all_to_all(traces, "rcv", split_axis=2, concat_axis=3, tiled=True)
    sectioned = regrouped.reshape(
        comp_count, freq_count, 1, local_rows // rcv_count, local_cols * rcv_count
    )
    arrived = lax.all_to_all(
        lax.all_to_all(sectioned, "src", split_axis=4, concat_axis=2, tiled=True),
        "rcv",
        split_axis=2,
        concat_axis=3,
        tiled=True,
    )
    mirrored = jnp.swapaxes(arrived.reshape(comp_count, freq_count, local_cols, local_rows), 2, 3)
    row_tiles = local_rows // TILE
    col_tiles = local_cols // TILE
    tile_mask = jnp.broadcast_to(
        missing[:, None, :, None] > 0, (row_tiles, TILE, col_tiles, TILE)
    ).reshape(local_rows, local_cols)
    filled = jnp.where(tile_mask[None, None], mirrored, traces)
    half_tile = TILE // half_count
    left_half = filled.reshape(comp_count, freq_count, local_rows, col_tiles, half_count, half_tile)
    left_half = lax.dynamic_index_in_dim(left_half, my_half, 4, keepdims=False)
    left_half = left_half.reshape(comp_count, freq_count, local_rows, col_tiles * half_tile)
    right_half = filled.reshape(
        comp_count, freq_count, row_tiles, half_count, half_tile, local_cols
    )
    right_half = lax.dynamic_index_in_dim(right_half, my_half, 3, keepdims=False)
    right_half = right_half.reshape(comp_count, freq_count, row_tiles * half_tile, local_cols)
    gathered = collect(left_half, "rcv", 3)
    block_count = gathered.shape[3] // half_tile
    chosen = (
        (aperture[:, :, None] == jnp.arange(block_count, dtype=jnp.int32)[None, None, :])
        .astype(jnp.float32)
        .sum(axis=1)
    )
    weighted = gathered.reshape(comp_count, freq_count, row_tiles, TILE, block_count, half_tile)
    weighted = (weighted * chosen[None, None, :, None, :, None]).reshape(
        comp_count, freq_count, local_rows, block_count * half_tile
    )
    slab_piece = lax.all_gather(right_half, "src", axis=2, tiled=True)
    real_part = complex_prod(weighted[0], slab_piece[0]) - complex_prod(weighted[1], slab_piece[1])
    imag_part = complex_prod(weighted[0], slab_piece[1]) + complex_prod(weighted[1], slab_piece[0])
    partial_sum = jnp.stack([real_part, imag_part])
    out_cols = local_cols // half_count
    my_share = sent_and_summed(partial_sum, "int", 3)
    kept_data = filled.reshape(comp_count, freq_count, local_rows, half_count, out_cols)
    kept_data = lax.dynamic_index_in_dim(kept_data, my_half, 3, keepdims=False)
    w_real = wavelet[0][:, None, None]
    w_imag = wavelet[1][:, None, None]
    out_real = kept_data[0] - (w_real * my_share[0] - w_imag * my_share[1])
    out_imag = kept_data[1] - (w_real * my_share[1] + w_imag * my_share[0])
    return jnp.stack([out_real, out_imag])


def solution(mesh):
    placed = (P(None, None, "src", "rcv"), P("src", "rcv"), P("src", None), P())
    return jax.shard_map(
        per_device,
        mesh=mesh,
        in_specs=placed,
        out_specs=P(None, None, "src", ("rcv", "int")),
        check_vma=False,
    )
```

profile of v0, /device:TPU:1, one launch (start us, length us, event | category | flops | bytes accessed | tf_op | source)
XLA Modules:
  0.0 221.6 jit_solution(6146417646936769049)
XLA Ops:
  6.5 1.4 copy.59
  8.0 26.7 %all_to_all.58 = f32[2,1,128,512]{3,0,1,2:T(2,128)S(1)} all-to-all(f32[2,1,128,512]{3,0,1,2:T(2,128)S(1)} %copy.59), channel_id=1, replica_groups=mesh['src'=32,'rcv'=8,'int'=2] {'rcv'}, dimensions={2} | all-to-all | bytes 1048576 | tf_op jit(solution)/shard_map/all_to_all | solution.py:45
  34.6 0.1 copy.60
  34.7 4.3 %copy.73 = f32[2,1,16,8,512]{2,0,4,3,1:T(2,128)} copy(f32[2,1,16,8,512]{4,2,3,0,1:T(8,128)S(1)} %bitcast.68) | data formatting | bytes 1048576 | tf_op jit(solution)/shard_map/reshape | solution.py:46
  39.0 7.3 %reshape.263 = f32[32,1,4096]{2,1,0:T(1,128)S(1)} reshape(f32[4096,1,1,2,16]{4,3,2,1,0:T(2,128)} %bitcast.59) | data formatting | bytes 1048576
  46.4 27.2 %all_to_all.59 = f32[32,1,4096]{2,1,0:T(1,128)S(1)} all-to-all(f32[32,1,4096]{2,1,0:T(1,128)S(1)} %reshape.263), channel_id=1, replica_groups=mesh['src'=32,'rcv'=8,'int'=2] {'src'}, dimensions={0} | all-to-all | bytes 1048576 | tf_op jit(solution)/shard_map/all_to_all | solution.py:50
  73.5 0.5 broadcast.100
  74.0 1.9 reduce.2
  75.9 0.0 copy-start
  75.9 6.9 %reshape.264 = f32[4096,1,1,2,16]{4,3,2,1,0:T(2,128)} reshape(f32[32,4096]{1,0:T(8,128)S(1)} %reduce.2) | data formatting | bytes 1048576
  82.9 0.0 copy-start.2
  82.9 5.9 %copy.63 = f32[2,1,1,16,32,128]{5,3,0,4,2,1:T(8,128)} copy(f32[2,1,1,16,32,128]{3,0,5,4,2,1:T(2,128)} %bitcast.60) | data formatting | bytes 1048576 | tf_op jit(solution)/shard_map/all_to_all | solution.py:50
  88.7 3.5 %all-to-all-start.2 = ((f32[2,1,32,16,128]{4,3,0,1,2:T(8,128)}), f32[2,1,32,16,128]{4,3,0,1,2:T(8,128)S(1)}, u32[]{:S(2)}, u32[]{:S(2)}) async-start(f32[2,1,32,16,128]{4,3,0,1,2:T(8,128)} %bitcast.7), calls=%async_computation.2 | async-start | bytes 1048576 | tf_op jit(solution)/shard_map/all_to_all | solution.py:49
  92.2 0.0 all-gather.3.cloned.1.call-start
  92.3 0.0 copy-done
  92.3 0.2 copy.66
  92.5 0.0 copy-done.2
  92.5 0.1 broadcast_bitcast_fusion
  92.6 15.9 %all-to-all-done.2 = f32[2,1,32,16,128]{4,3,0,1,2:T(8,128)S(1)} async-done(((f32[2,1,32,16,128]{4,3,0,1,2:T(8,128)}), f32[2,1,32,16,128]{4,3,0,1,2:T(8,128)S(1)}, u32[]{:S(2)}, u32[]{:S(2)}) %all-to-all-start.2) | async-done | bytes 524320 | tf_op jit(solution)/shard_map/all_to_all | solution.py:49
  108.6 0.1 bitcast_select_fusion
  108.7 0.2 copy.69
  108.9 0.0 copy-start.3
  108.9 0.7 constant_dynamic-slice_fusion.1
  109.7 0.0 all-gather.3.cloned.1.call-update
  109.7 1.6 broadcast_in_dim.25
  111.3 3.8 %all-to-all-start.3 = ((f32[8,2,1,128,256]{3,4,1,2,0:T(8,128)}), f32[8,2,1,128,256]{3,4,1,2,0:T(8,128)S(1)}, u32[]{:S(2)}, u32[]{:S(2)}) async-start(f32[8,2,1,128,256]{3,4,1,2,0:T(8,128)} %broadcast_in_dim.25), calls=%async_computation.3 | async-start | bytes 4194304 | tf_op jit(solution)/shard_map/all_to_all | solution.py:11
  115.1 0.0 copy-done.3
  115.1 0.1 convert_reduce_fusion
  115.2 48.5 %all-to-all-done.3 = f32[8,2,1,128,256]{3,4,1,2,0:T(8,128)S(1)} async-done(((f32[8,2,1,128,256]{3,4,1,2,0:T(8,128)}), f32[8,2,1,128,256]{3,4,1,2,0:T(8,128)S(1)}, u32[]{:S(2)}, u32[]{:S(2)}) %all-to-all-start.3) | async-done | bytes 2097184 | tf_op jit(solution)/shard_map/all_to_all | solution.py:11
  163.7 0.2 copy.68
  163.9 0.2 broadcast_multiply_fusion
  164.1 0.2 fusion.6
  164.3 14.9 %all-gather.3.cloned.1.call-done = f32[2,1,1,1,2048,512]{5,4,3,0,2,1:T(8,128)} async-done(((f32[2,1,1,1,64,512]{5,4,3,0,2,1:T(8,128)}), f32[2,1,1,1,2048,512]{5,4,3,0,2,1:T(8,128)}) %all-gather.3.cloned.1.call-update) | async-done | bytes 8388624 | tf_op jit(solution)/shard_map/all_gather | solution.py:83
  179.2 4.8 %fusion = f32[128,512]{1,0:T(8,128)S(1)} fusion(f32[128,2048]{0,1:T(8,128)S(1)} %bitcast.61, f32[2,1,1,1,2048,512]{5,4,3,0,2,1:T(8,128)} %all-gather.3.cloned.1.call-done), kind=kOutput, calls=%fused_computation.2 | convolution fusion | flops 1610612736 | bytes 5505024 | tf_op jit(solution)/shard_map/fik,fkj->fij/dot_general | solution.py:37
  184.0 4.8 %fusion.5 = f32[128,512]{1,0:T(8,128)S(1)} fusion(f32[128,512]{1,0:T(8,128)S(1)} %fusion, f32[128,2048]{0,1:T(8,128)S(1)} %bitcast.63, f32[2,1,1,1,2048,512]{5,4,3,0,2,1:T(8,128)} %all-gather.3.cloned.1.call-done), kind=kOutput, calls=%fused_computation.7 | convolution fusion | flops 1610678272 | bytes 5767168 | tf_op jit(solution)/shard_map/fik,fkj->fij/dot_general | solution.py:37
  188.8 0.2 stack.15
  189.0 4.8 %fusion.1 = f32[128,512]{1,0:T(8,128)S(1)} fusion(f32[128,2048]{0,1:T(8,128)S(1)} %bitcast.64, f32[2,1,1,1,2048,512]{5,4,3,0,2,1:T(8,128)} %all-gather.3.cloned.1.call-done), kind=kOutput, calls=%fused_computation.3 | convolution fusion | flops 1610612736 | bytes 5505024 | tf_op jit(solution)/shard_map/fik,fkj->fij/dot_general | solution.py:37
  193.8 0.0 copy-start.1
  193.8 4.8 %fusion.4 = f32[128,512]{1,0:T(8,128)S(1)} fusion(f32[128,512]{1,0:T(8,128)S(1)} %fusion.1, f32[128,2048]{0,1:T(8,128)S(1)} %bitcast.62, f32[2,1,1,1,2048,512]{5,4,3,0,2,1:T(8,128)} %all-gather.3.cloned.1.call-done), kind=kOutput, calls=%fused_computation.6 | convolution fusion | flops 1610678272 | bytes 5767168 | tf_op jit(solution)/shard_map/fik,fkj->fij/dot_general | solution.py:37
  198.6 0.2 stack.14
  198.8 0.8 maximum_bitcast_fusion
  199.6 4.0 %all-to-all-start.4 = ((f32[2,2,1,128,256]{4,3,2,1,0:T(8,128)}), f32[2,2,1,128,256]{4,3,2,1,0:T(8,128)S(1)}, u32[]{:S(2)}, u32[]{:S(2)}) async-start(f32[2,2,1,128,256]{4,3,2,1,0:T(8,128)} %maximum_bitcast_fusion), calls=%async_computation.4 | async-start | bytes 1048576 | tf_op jit(solution)/shard_map/all_to_all | solution.py:32
  203.6 0.0 copy-done.1
  203.6 0.6 fusion.7
  204.3 0.1 copy.77
  204.4 0.1 copy.80
  204.5 8.2 %all-to-all-done.4 = f32[2,2,1,128,256]{4,3,2,1,0:T(8,128)S(1)} async-done(((f32[2,2,1,128,256]{4,3,2,1,0:T(8,128)}), f32[2,2,1,128,256]{4,3,2,1,0:T(8,128)S(1)}, u32[]{:S(2)}, u32[]{:S(2)}) %all-to-all-start.4) | async-done | bytes 524320 | tf_op jit(solution)/shard_map/all_to_all | solution.py:32
  212.7 1.3 bitcast_subtract_fusion.1
  214.0 0.7 pad_maximum_fusion
  (8 shorter events, 0.2 us)
Async XLA Ops:
  75.9 16.3 %copy-start = (f32[2,1,128,512]{3,2,1,0:T(8,128)S(1)}, f32[2,1,128,512]{3,2,1,0:T(8,128)}, u32[]{:S(2)}) copy-start(f32[2,1,128,512]{3,2,1,0:T(8,128)} %param.4) | copy-start | bytes 1572868
  82.9 9.6 %copy-start.2 = (s32[1,4]{1,0:T(1,128)S(1)}, s32[1,4]{1,0:T(1,128)}, u32[]{:S(2)}) copy-start(s32[1,4]{1,0:T(1,128)} %param.5) | copy-start | bytes 52
  88.7 19.8 %all-to-all-start.2 = ((f32[2,1,32,16,128]{4,3,0,1,2:T(8,128)}), f32[2,1,32,16,128]{4,3,0,1,2:T(8,128)S(1)}, u32[]{:S(2)}, u32[]{:S(2)}) async-start(f32[2,1,32,16,128]{4,3,0,1,2:T(8,128)} %bitcast.7), calls=%async_computation.2 | async-start | bytes 1048576 | tf_op jit(solution)/shard_map/all_to_all | solution.py:49
  92.2 87.0 %all-gather.3.cloned.1.call-start = ((), (), s32[]{:S(2)}) async-start(), calls=%async_computation.5 | async-start | bytes 8650752 | tf_op jit(solution)/shard_map/all_gather | solution.py:83
  108.9 6.2 %copy-start.3 = (s32[1,24]{1,0:T(1,128)S(1)}, s32[1,24]{1,0:T(1,128)}, u32[]{:S(2)}) copy-start(s32[1,24]{1,0:T(1,128)} %param.6) | copy-start | bytes 292
  111.3 52.4 %all-to-all-start.3 = ((f32[8,2,1,128,256]{3,4,1,2,0:T(8,128)}), f32[8,2,1,128,256]{3,4,1,2,0:T(8,128)S(1)}, u32[]{:S(2)}, u32[]{:S(2)}) async-start(f32[8,2,1,128,256]{3,4,1,2,0:T(8,128)} %broadcast_in_dim.25), calls=%async_computation.3 | async-start | bytes 4194304 | tf_op jit(solution)/shard_map/all_to_all | solution.py:11
  193.8 9.8 %copy-start.1 = (f32[2,1]{0,1:T(1,128)S(1)}, f32[2,1]{0,1:T(1,128)}, u32[]{:S(2)}) copy-start(f32[2,1]{0,1:T(1,128)} %param.7) | copy-start | bytes 28
  199.6 13.0 %all-to-all-start.4 = ((f32[2,2,1,128,256]{4,3,2,1,0:T(8,128)}), f32[2,2,1,128,256]{4,3,2,1,0:T(8,128)S(1)}, u32[]{:S(2)}, u32[]{:S(2)}) async-start(f32[2,2,1,128,256]{4,3,2,1,0:T(8,128)} %maximum_bitcast_fusion), calls=%async_computation.4 | async-start | bytes 1048576 | tf_op jit(solution)/shard_map/all_to_all | solution.py:32
Sparse Core Ops, SparseCore 0:
  109.8 69.3 all-gather.2
where the time goes:
time: 222 us
  waiting for transfers between devices  87.5 us (39%)
  blocking collectives  53.8 us (24%)
  local copies, waits for them, and re-layouts  30.9 us (14%)
  matrix products  19.2 us (9%)
  between operations  13.7 us (6%)
  starting transfers between devices  11.3 us (5%)
  other arithmetic  5.23 us (2%)
    all_to_all x1, waiting for transfers between devices, from_everyone(): return lax.all_to_all(copies, axis, split_axis=0, concat_axis=0, tiled=True)  48.5 us
    all_to_all x1, blocking collectives, per_device(): lax.all_to_all(sectioned, 'src', split_axis=4, concat_axis=2, tiled=True)  27.2 us
    all_to_all x1, blocking collectives, per_device(): lax.all_to_all(traces, 'rcv', split_axis=2, concat_axis=3, tiled=True)  26.7 us
    dot_general x4, matrix products, complex_prod(): jnp.einsum('fik,fkj->fij', left_side, right_side, precision=lax.Precision...  19.2 us
    unnamed x14, local copies, waits for them, and re-layouts  16.1 us
    all_to_all x1, waiting for transfers between devices, per_device(): lax.all_to_all(lax.all_to_all(sectioned, 'src', split_axis=4, concat_axis...  15.9 us
    all_gather x1, waiting for transfers between devices, per_device(): slab_piece = lax.all_gather(right_half, 'src', axis=2, tiled=True)  14.9 us
    all_to_all x1, waiting for transfers between devices, sent_and_summed(): lax.all_to_all(pieces, axis, split_axis=0, concat_axis=0, tiled=True)  8.19 us
  transfers between devices with their start and end apart: 4, of which 4 were waited for; matrix products, arithmetic and copies ran while one was open for 2% of the time, Pallas kernels for 0%

commit v1 on v0

--- a/solution.py
+++ b/solution.py
@@ -80,7 +80,9 @@
     weighted = (weighted * chosen[None, None, :, None, :, None]).reshape(
         comp_count, freq_count, local_rows, block_count * half_tile
     )
-    slab_piece = lax.all_gather(right_half, "src", axis=2, tiled=True)
+    slab_piece = jnp.concatenate(
+        lax.all_to_all(jnp.stack([right_half] * lax.axis_size("src")), "src", 0, 0), axis=2
+    )
     real_part = complex_prod(weighted[0], slab_piece[0]) - complex_prod(weighted[1], slab_piece[1])
     imag_part = complex_prod(weighted[0], slab_piece[1]) + complex_prod(weighted[1], slab_piece[0])
     partial_sum = jnp.stack([real_part, imag_part])

time: 222 us -> 389 us (1.75)
  waiting for transfers between devices: 87.5 us -> 261 us
  between operations: 13.7 us -> 0.31 us
  local copies, waits for them, and re-layouts: 30.9 us -> 39 us
  matrix products: 19.2 us -> 12.8 us
  starting transfers between devices: 11.3 us -> 16.2 us
    all_to_all x0 -> x1, waiting for transfers between devices: none -> 186 us  [per_device(): lax.all_to_all(jnp.stack([right_half] * lax.axis_size('src')), 'src', 0, 0)]
    all_gather x1 -> x0, waiting for transfers between devices: 14.9 us -> none  [per_device(): slab_piece = lax.all_gather(right_half, 'src', axis=2, tiled=True)]
    dot_general x4, matrix products: 19.2 us -> 12.8 us  [complex_prod(): jnp.einsum('fik,fkj->fij', left_side, right_side, precision=lax.Precision...]
    all_to_all x0 -> x1, starting transfers between devices: none -> 5.4 us  [per_device(): lax.all_to_all(jnp.stack([right_half] * lax.axis_size('src')), 'src', 0, 0)]
    slice x1 -> x2, local copies, waits for them, and re-layouts: 0.24 us -> 4.77 us  [the longest x1 4.53 us: per_device(): slab_piece[0]]
    another operation x0 -> x2, local copies, waits for them, and re-layouts: none -> 4.33 us  [per_device(): jnp.stack([right_half] * lax.axis_size('src'))]
    unnamed x14 -> x16, local copies, waits for them, and re-layouts: 16.1 us -> 16.1 us
  transfers between devices with their start and end apart: 4 -> 4, of which waited for: 4 -> 4; matrix products, arithmetic and copies ran while one was open for 2% -> 1% of each run, Pallas kernels for 0% -> 0%
where the time goes in v1:
time: 389 us; the launch traced here: 388 us
  waiting for transfers between devices  261 us (67%)
  blocking collectives  53.8 us (14%)
  local copies, waits for them, and re-layouts  39 us (10%)
  starting transfers between devices  16.2 us (4%)
  matrix products  12.8 us (3%)
  other arithmetic  5.24 us (1%)
    all_to_all x1, waiting for transfers between devices, per_device(): lax.all_to_all(jnp.stack([right_half] * lax.axis_size('src')), 'src', 0, 0)  186 us
    all_to_all x1, waiting for transfers between devices, from_everyone(): return lax.all_to_all(copies, axis, split_axis=0, concat_axis=0, tiled=True)  51.3 us
    all_to_all x1, blocking collectives, per_device(): lax.all_to_all(sectioned, 'src', split_axis=4, concat_axis=2, tiled=True)  27.2 us
    all_to_all x1, blocking collectives, per_device(): lax.all_to_all(traces, 'rcv', split_axis=2, concat_axis=3, tiled=True)  26.7 us
    unnamed x16, local copies, waits for them, and re-layouts  16.1 us
    all_to_all x1, waiting for transfers between devices, per_device(): lax.all_to_all(lax.all_to_all(sectioned, 'src', split_axis=4, concat_axis...  16 us
    dot_general x4, matrix products, complex_prod(): jnp.einsum('fik,fkj->fij', left_side, right_side, precision=lax.Precision...  12.8 us
    all_to_all x1, waiting for transfers between devices, sent_and_summed(): lax.all_to_all(pieces, axis, split_axis=0, concat_axis=0, tiled=True)  7.98 us
  transfers between devices with their start and end apart: 4, of which 4 were waited for; matrix products, arithmetic and copies ran while one was open for 1% of the time, Pallas kernels for 0%

profile of v1, /device:TPU:1, one launch (start us, length us, event | category | flops | bytes accessed | tf_op | source)
XLA Modules:
  0.0 388.4 jit_solution(4078978380341721298)
XLA Ops:
  0.0 1.4 copy.59
  1.4 26.7 %all_to_all.63 = f32[2,1,128,512]{3,0,1,2:T(2,128)S(1)} all-to-all(f32[2,1,128,512]{3,0,1,2:T(2,128)S(1)} %copy.59), channel_id=1, replica_groups=mesh['src'=32,'rcv'=8,'int'=2] {'rcv'}, dimensions={2} | all-to-all | bytes 1048576 | tf_op jit(solution)/shard_map/all_to_all | solution.py:45
  28.1 0.1 copy.60
  28.2 4.3 %copy.73 = f32[2,1,16,8,512]{2,0,4,3,1:T(2,128)} copy(f32[2,1,16,8,512]{4,2,3,0,1:T(8,128)S(1)} %bitcast.69) | data formatting | bytes 1048576 | tf_op jit(solution)/shard_map/reshape | solution.py:46
  32.5 7.3 %reshape.267 = f32[32,1,4096]{2,1,0:T(1,128)S(1)} reshape(f32[4096,1,1,2,16]{4,3,2,1,0:T(2,128)} %bitcast.60) | data formatting | bytes 1048576
  39.8 27.2 %all_to_all.64 = f32[32,1,4096]{2,1,0:T(1,128)S(1)} all-to-all(f32[32,1,4096]{2,1,0:T(1,128)S(1)} %reshape.267), channel_id=1, replica_groups=mesh['src'=32,'rcv'=8,'int'=2] {'src'}, dimensions={0} | all-to-all | bytes 1048576 | tf_op jit(solution)/shard_map/all_to_all | solution.py:50
  67.0 0.5 broadcast.102
  67.5 1.9 reduce.2
  69.4 0.0 copy-start.1
  69.4 6.9 %reshape.268 = f32[4096,1,1,2,16]{4,3,2,1,0:T(2,128)} reshape(f32[32,4096]{1,0:T(8,128)S(1)} %reduce.2) | data formatting | bytes 1048576
  76.3 0.0 copy-start.3
  76.3 5.8 %copy.63 = f32[2,1,1,16,32,128]{5,3,0,4,2,1:T(8,128)} copy(f32[2,1,1,16,32,128]{3,0,5,4,2,1:T(2,128)} %bitcast.61) | data formatting | bytes 1048576 | tf_op jit(solution)/shard_map/all_to_all | solution.py:50
  82.2 3.5 all-to-all-start.2
  85.7 0.0 copy-done.1
  85.7 0.2 copy.66
  85.9 0.0 copy-done.3
  85.9 0.1 broadcast_bitcast_fusion
  86.0 16.0 %all-to-all-done.2 = f32[2,1,32,16,128]{4,3,0,1,2:T(8,128)S(1)} async-done(((f32[2,1,32,16,128]{4,3,0,1,2:T(8,128)}), f32[2,1,32,16,128]{4,3,0,1,2:T(8,128)S(1)}, u32[]{:S(2)}, u32[]{:S(2)}) %all-to-all-start.2) | async-done | bytes 524320 | tf_op jit(solution)/shard_map/all_to_all | solution.py:49
  102.0 0.1 bitcast_select_fusion
  102.2 1.5 broadcast_in_dim.25
  103.8 3.6 all-to-all-start.3
  107.4 0.2 copy.69
  107.6 51.3 %all-to-all-done.3 = f32[8,2,1,128,256]{3,4,1,2,0:T(8,128)S(1)} async-done(((f32[8,2,1,128,256]{3,4,1,2,0:T(8,128)}), f32[8,2,1,128,256]{3,4,1,2,0:T(8,128)S(1)}, u32[]{:S(2)}, u32[]{:S(2)}) %all-to-all-start.3) | async-done | bytes 2097184 | tf_op jit(solution)/shard_map/all_to_all | solution.py:11
  159.0 4.3 %stack.17 = f32[32,2,1,64,512]{4,3,2,1,0:T(8,128)} broadcast(f32[2,64,512]{2,1,0:T(8,128)S(1)} %dynamic-slice_bitcast_fusion), dimensions={1,3,4} | broadcast | bytes 8650752 | tf_op jit(solution)/shard_map/stack | solution.py:84
  163.3 0.0 copy-start.4
  163.3 5.4 %all-to-all-start.4 = ((f32[32,2,1,64,512]{4,3,2,1,0:T(8,128)}), f32[32,2,1,64,512]{4,3,2,1,0:T(8,128)}, u32[]{:S(2)}, u32[]{:S(2)}) async-start(f32[32,2,1,64,512]{4,3,2,1,0:T(8,128)} %stack.17), calls=%async_computation.4 | async-start | bytes 16777216 | tf_op jit(solution)/shard_map/all_to_all | solution.py:84
  168.7 0.0 copy-done.4
  168.7 0.1 convert_reduce_fusion
  168.8 0.2 copy.68
  168.9 0.2 broadcast_multiply_fusion
  169.1 0.2 fusion.1
  169.4 185.8 %all-to-all-done.4 = f32[32,2,1,64,512]{4,3,2,1,0:T(8,128)} async-done(((f32[32,2,1,64,512]{4,3,2,1,0:T(8,128)}), f32[32,2,1,64,512]{4,3,2,1,0:T(8,128)}, u32[]{:S(2)}, u32[]{:S(2)}) %all-to-all-start.4) | async-done | bytes 8388640 | tf_op jit(solution)/shard_map/all_to_all | solution.py:84
  355.2 4.5 %fusion = (f32[1,1,32,64,512]{4,3,1,0,2:T(8,128)S(1)}, f32[1,1,32,64,512]{4,3,1,0,2:T(8,128)S(1)}) fusion(f32[2,1,32,64,512]{4,3,1,0,2:T(8,128)} %bitcast.23), kind=kLoop, calls=%fused_computation.16 | loop fusion | bytes 16777216 | tf_op jit(solution)/shard_map/slice | solution.py:86
  359.7 0.0 copy-start
  359.7 2.7 fusion.3
  362.4 2.7 fusion.4
  365.1 0.0 copy-done
  365.1 2.7 convolution_subtract_fusion
  367.8 0.2 stack.18
  368.0 0.0 copy-start.2
  368.0 4.8 %convolution_add_fusion = f32[128,512]{1,0:T(8,128)S(1)} fusion(f32[128,512]{1,0:T(8,128)S(1)} %fusion.4, f32[128,2048]{0,1:T(8,128)S(1)} %bitcast.63, f32[2048,512]{1,0:T(8,128)} %bitcast.57), kind=kOutput, calls=%fused_computation | convolution fusion | flops 1610678272 | bytes 5767168 | tf_op jit(solution)/shard_map/fik,fkj->fij/dot_general | solution.py:37
  372.8 0.2 stack.19
  373.0 0.8 maximum_bitcast_fusion
  373.8 3.7 all-to-all-start.5
  377.5 0.0 copy-done.2
  377.5 0.6 fusion.2
  378.2 0.1 copy.77
  378.3 0.1 copy.80
  378.4 8.0 %all-to-all-done.5 = f32[2,2,1,128,256]{4,3,2,1,0:T(8,128)S(1)} async-done(((f32[2,2,1,128,256]{4,3,2,1,0:T(8,128)}), f32[2,2,1,128,256]{4,3,2,1,0:T(8,128)S(1)}, u32[]{:S(2)}, u32[]{:S(2)}) %all-to-all-start.5) | async-done | bytes 524320 | tf_op jit(solution)/shard_map/all_to_all | solution.py:32
  386.4 1.3 bitcast_subtract_fusion.1
  387.7 0.7 pad_maximum_fusion
  (9 shorter events, 0.2 us)
Async XLA Ops:
  69.4 16.3 %copy-start.1 = (f32[2,1,128,512]{3,2,1,0:T(8,128)S(1)}, f32[2,1,128,512]{3,2,1,0:T(8,128)}, u32[]{:S(2)}) copy-start(f32[2,1,128,512]{3,2,1,0:T(8,128)} %param.4) | copy-start | bytes 1572868
  76.3 9.6 %copy-start.3 = (s32[1,4]{1,0:T(1,128)S(1)}, s32[1,4]{1,0:T(1,128)}, u32[]{:S(2)}) copy-start(s32[1,4]{1,0:T(1,128)} %param.5) | copy-start | bytes 52
  82.2 19.8 %all-to-all-start.2 = ((f32[2,1,32,16,128]{4,3,0,1,2:T(8,128)}), f32[2,1,32,16,128]{4,3,0,1,2:T(8,128)S(1)}, u32[]{:S(2)}, u32[]{:S(2)}) async-start(f32[2,1,32,16,128]{4,3,0,1,2:T(8,128)} %bitcast.7), calls=%async_computation.2 | async-start | bytes 1048576 | tf_op jit(solution)/shard_map/all_to_all | solution.py:49
  103.8 55.2 %all-to-all-start.3 = ((f32[8,2,1,128,256]{3,4,1,2,0:T(8,128)}), f32[8,2,1,128,256]{3,4,1,2,0:T(8,128)S(1)}, u32[]{:S(2)}, u32[]{:S(2)}) async-start(f32[8,2,1,128,256]{3,4,1,2,0:T(8,128)} %broadcast_in_dim.25), calls=%async_computation.3 | async-start | bytes 4194304 | tf_op jit(solution)/shard_map/all_to_all | solution.py:11
  163.3 5.4 %copy-start.4 = (s32[1,24]{1,0:T(1,128)S(1)}, s32[1,24]{1,0:T(1,128)}, u32[]{:S(2)}) copy-start(s32[1,24]{1,0:T(1,128)} %param.6) | copy-start | bytes 292
  163.3 191.9 %all-to-all-start.4 = ((f32[32,2,1,64,512]{4,3,2,1,0:T(8,128)}), f32[32,2,1,64,512]{4,3,2,1,0:T(8,128)}, u32[]{:S(2)}, u32[]{:S(2)}) async-start(f32[32,2,1,64,512]{4,3,2,1,0:T(8,128)} %stack.17), calls=%async_computation.4 | async-start | bytes 16777216 | tf_op jit(solution)/shard_map/all_to_all | solution.py:84
  359.7 5.3 %copy-start = (f32[1,1,32,64,512]{4,3,1,0,2:T(8,128)}, f32[1,1,32,64,512]{4,3,1,0,2:T(8,128)S(1)}, u32[]{:S(2)}) copy-start(f32[1,1,32,64,512]{4,3,1,0,2:T(8,128)S(1)} %get-tuple-element.5) | copy-start | bytes 12582916
  368.0 9.6 %copy-start.2 = (f32[2,1]{0,1:T(1,128)S(1)}, f32[2,1]{0,1:T(1,128)}, u32[]{:S(2)}) copy-start(f32[2,1]{0,1:T(1,128)} %param.7) | copy-start | bytes 28
  373.8 12.5 %all-to-all-start.5 = ((f32[2,2,1,128,256]{4,3,2,1,0:T(8,128)}), f32[2,2,1,128,256]{4,3,2,1,0:T(8,128)S(1)}, u32[]{:S(2)}, u32[]{:S(2)}) async-start(f32[2,2,1,128,256]{4,3,2,1,0:T(8,128)} %maximum_bitcast_fusion), calls=%async_computation.5 | async-start | bytes 1048576 | tf_op jit(solution)/shard_map/all_to_all | solution.py:32
